TPU v7x, 32 devices: a whole 2x2x4 slice. The times are simulated.
32 devices in a mesh: seq: 4 (over z), ch: 8 (over y, x, core).
Axes of the slice: x: 2, y: 2, z: 4, core: 2. Of those that a mesh axis runs over, the one named last changes fastest.
Arguments:
- inputs: bfloat16 [1024, 8192], P('seq', 'ch'), may hold values from -6 to 6
- w_in: bfloat16 [3, 8192, 8192], P(None, 'seq', 'ch'), may hold values from -0.0625 to 0.0625
- short_filter: float32 [3, 3, 8192], P(None, None, 'ch'), may hold values from -3 to 3
- rates: float32 [16, 8192], P(None, 'ch'), may hold values from 9.765625e-05 to 0.05
- residues: float32 [16, 8192], P(None, 'ch'), may hold values from -3 to 3
- skip: float32 [8192], P('ch'), may hold values from -3 to 3
Outputs:
- gated: bfloat16 [1024, 8192], P('seq', 'ch')
All inputs are finite; a program needn't handle non-finite values.
Results may differ from a plain program's by a relative error of at most 0.0065.
Values may be sent and summed in bfloat16 or wider, within the bound.
No kernel may reach another device: no remote copies, remote signals or barrier semaphores. Data moves between devices by JAX's collectives and lax.ppermute only.
A program may use at most 128 MiB of HBM per device.

v0:
```python
import jax
import jax.numpy as jnp
from jax import lax
from jax.sharding import PartitionSpec as P

TAPS = 3


def passed_along(block, axis, distance):
    devices = range(lax.axis_size(axis))
    route = [(i - distance, i) for i in devices if i - distance in devices]
    return lax.ppermute(block, axis, route)


def carried_in(part, axis, combine, identity):
    place = lax.axis_index(axis)
    gathered = jax.tree.map(lambda a: lax.all_gather(a, axis), part)
    state = jax.tree.map(lambda a, e: jnp.zeros_like(a) + jnp.asarray(e, a.dtype), part, identity)

    def one(hop, state):
        return combine(
            state, jax.tree.map(lambda a: lax.dynamic_index_in_dim(a, hop, 0, False), gathered)
        )

    return lax.fori_loop(0, place, one, state)


def combine(earlier, later):
    return (earlier[0] * later[0], earlier[1] * later[0] + later[1])


def per_device(inputs, w_in, short_filter, rates, residues, skip):
    tok_rows = inputs.shape[0]
    width = w_in.shape[2]
    modes = rates.shape[0]
    features = lax.all_gather(inputs, "ch", axis=1, tiled=True)
    proj = jnp.einsum(
        "td,kdc->ktc",
        features,
        lax.all_gather(w_in, "seq", axis=1, tiled=True),
        preferred_element_type=jnp.float32,
    ).astype(jnp.bfloat16)
    prior = passed_along(proj[:, tok_rows - (TAPS - 1) :, :], "seq", 1)
    padded = jnp.concatenate([prior, proj], axis=1).astype(jnp.float32)
    mixed = jnp.zeros((3, tok_rows, width), jnp.float32)
    for j in range(TAPS):
        mixed = (
            mixed
            + short_filter[:, j, None, :] * padded[:, TAPS - 1 - j : TAPS - 1 - j + tok_rows, :]
        )
    query, key, value = (mixed[0], mixed[1], mixed[2])
    drive = key * value
    position = jnp.arange(tok_rows, dtype=jnp.float32)
    scaled = residues * jnp.sqrt(1.0 - jnp.exp(-2.0 * rates))
    end_powers = jnp.exp(-rates[None, :, :] * (tok_rows - 1.0 - position)[:, None, None])
    end_state = jnp.sum(end_powers * drive[:, None, :], axis=0)
    block_decay = jnp.exp(-rates * tok_rows)
    identity = (jnp.ones_like(block_decay), jnp.zeros_like(end_state))
    entering = carried_in((block_decay, end_state), "seq", combine, identity)[1]
    start_powers = jnp.exp(-rates[None, :, :] * (position + 1.0)[:, None, None])
    cross = jnp.sum(start_powers * (scaled * entering)[None, :, :], axis=1)
    center = (tok_rows - 1.0) / 2.0
    offset = (position - center)[:, None, None]
    rising = jnp.exp(rates[None, :, :] * offset) * drive[:, None, :]
    offsets = jnp.arange(tok_rows, dtype=jnp.int32)
    lower = (offsets[:, None] >= offsets[None, :]).astype(jnp.float32)
    prefix = jnp.dot(
        lower, rising.reshape(tok_rows, modes * width), precision=lax.Precision.HIGHEST
    )
    prefix = prefix.reshape(tok_rows, modes, width)
    falling = jnp.exp(-rates[None, :, :] * offset) * scaled[None, :, :]
    local = jnp.sum(falling * prefix, axis=1)
    return (query * (local + cross + skip[None, :] * drive)).astype(jnp.bfloat16)


def solution(mesh):
    in_specs = (
        P("seq", "ch"),
        P(None, "seq", "ch"),
        P(None, None, "ch"),
        P(None, "ch"),
        P(None, "ch"),
        P("ch"),
    )
    out_specs = P("seq", "ch")
    return jax.shard_map(
        per_device, mesh=mesh, in_specs=in_specs, out_specs=out_specs, check_vma=False
    )
```

profile of v0, /device:TPU:0, one launch (start us, length us, event | category | flops | bytes accessed | tf_op | source)
XLA Modules:
  0.0 979.4 jit_solution(17450163939474768816)
XLA Ops:
  6.5 0.0 all-gather.7.cloned.1.call-start
  6.5 0.7 all-gather.7.cloned.1.call-update
  7.3 0.0 all-gather.5.cloned.1.call-start
  7.3 0.7 all-gather.5.cloned.1.call-update
  8.0 0.9 fusion.17
  9.0 1.5 fusion.16
  10.5 0.0 copy-start
  10.5 38.1 %all-gather.7.cloned.1.call-done = bf16[256,8192]{1,0:T(8,128)(2,1)} async-done(((bf16[256,1024]{1,0:T(8,128)(2,1)}), bf16[256,8192]{1,0:T(8,128)(2,1)}) %all-gather.7.cloned.1.call-update) | async-done | bytes 4194320 | tf_op jit(solution)/shard_map/all_gather | solution.py:36
  48.6 837.6 %all-gather.5.cloned.1.call-done = bf16[3,8192,1024]{2,1,0:T(8,128)(2,1)} async-done(((bf16[3,2048,1024]{2,1,0:T(8,128)(2,1)}), bf16[3,8192,1024]{2,1,0:T(8,128)(2,1)}) %all-gather.5.cloned.1.call-update) | async-done | bytes 50331664 | tf_op jit(solution)/shard_map/all_gather | solution.py:40
  886.2 21.8 %fusion.7 = bf16[3,256,1024]{2,1,0:T(8,128)(2,1)S(1)} fusion(bf16[3,8192,1024]{2,1,0:T(8,128)(2,1)} %all-gather.5.cloned.1.call-done, bf16[256,8192]{1,0:T(8,128)(2,1)} %all-gather.7.cloned.1.call-done), kind=kOutput, calls=%fused_computation.15 | convolution fusion | flops 12885688320 | bytes 56098816 | tf_op jit(solution)/shard_map/td,kdc->ktc/dot_general | solution.py:37
  908.0 1.3 collective-permute-start
  909.3 14.3 %all-gather = f32[64,1024]{1,0:T(8,128)S(1)} all-gather(f32[16,1024]{1,0:T(8,128)S(1)} %get-tuple-element.63), channel_id=2, replica_groups=mesh['seq'=4,'ch'=8] {'seq'}, dimensions={0}, use_global_device_ids=true | all-gather | bytes 327680 | tf_op jit(solution)/shard_map/all_gather | solution.py:17
  923.6 0.0 copy-done
  923.6 0.6 copy.13
  924.3 0.0 collective-permute-done
  924.3 0.5 maximum_convert_fusion
  924.7 0.9 fusion.2
  925.7 1.2 fusion.10
  926.8 2.5 copy.12
  929.4 4.1 multiply_reduce_fusion.1
  933.5 14.6 %all-gather.1 = f32[64,1024]{1,0:T(8,128)} all-gather(f32[16,1024]{1,0:T(8,128)S(1)} %multiply_reduce_fusion.1), channel_id=3, replica_groups=mesh['seq'=4,'ch'=8] {'seq'}, dimensions={0}, use_global_device_ids=true | all-gather | bytes 327680 | tf_op jit(solution)/shard_map/all_gather | solution.py:17
  948.1 0.2 while.12
  948.3 0.0 copy-start.1
  948.3 0.9 fusion.15
  949.2 3.9 bitcast_multiply_fusion.1
  953.1 0.0 copy-start.2
  953.1 0.0 copy-done.1
  953.1 14.0 %multiply_reduce_fusion.2 = f32[256,1024]{1,0:T(8,128)} fusion(f32[16,1024,256]{2,1,0:T(8,128)S(1)} %bitcast.50, f32[16,1024]{1,0:T(8,128)S(1)} %get-tuple-element.61, f32[256]{0:T(256)S(1)} %iota_add_fusion.1, f32[16,1024]{1,0:T(8,128)S(1)} %copy-done.1), kind=kOutput, calls=%fused_computation.5 | convolution fusion | flops 12901482496 | bytes 17957888 | tf_op jit(solution)/shard_map/dot_general | solution.py:67
  967.2 2.8 multiply_reduce_fusion
  970.0 0.0 copy-done.2
  970.0 2.6 fusion.12
  (7 shorter events, 0.1 us)
Async XLA Ops:
  6.5 42.0 %all-gather.7.cloned.1.call-start = ((), (), s32[]{:S(2)}) async-start(), calls=%async_computation.1 | async-start | bytes 4718592 | tf_op jit(solution)/shard_map/all_gather | solution.py:36
  7.3 878.9 %all-gather.5.cloned.1.call-start = ((), (), s32[]{:S(2)}) async-start(), calls=%async_computation | async-start | bytes 62914560 | tf_op jit(solution)/shard_map/all_gather | solution.py:40
  10.5 913.1 %copy-start = (f32[16,1024]{1,0:T(8,128)S(1)}, f32[16,1024]{1,0:T(8,128)}, u32[]{:S(2)}) copy-start(f32[16,1024]{1,0:T(8,128)} %param.11) | copy-start | bytes 196612
  908.0 16.3 %collective-permute-start = (bf16[3,2,1024]{2,1,0:T(2,128)(2,1)S(1)}, bf16[3,2,1024]{2,1,0:T(2,128)(2,1)S(1)}, u32[]{:S(2)}, u32[]{:S(2)}) collective-permute-start(bf16[3,2,1024]{2,1,0:T(2,128)(2,1)S(1)} %slice.40), channel_id=1, source_target_pairs={{0,8},{8,16},{16,24},{1,9},{9,17},{17,25},{2,10},{10,18},{18,26},{... | collective-permute-start | bytes 36872 | tf_op jit(solution)/shard_map/ppermute | solution.py:12
  948.3 4.8 copy-start.1
  953.1 16.9 %copy-start.2 = (f32[1024]{0:T(1024)S(1)}, f32[1024]{0:T(1024)}, u32[]{:S(2)}) copy-start(f32[1024]{0:T(1024)} %param.13) | copy-start | bytes 12292
Sparse Core Ops, SparseCore 0:
  9.2 39.2 all-gather.6
  50.1 835.9 all-gather.4
where the time goes:
time: 980 us; the launch traced here: 979 us
  waiting for transfers between devices  877 us (89%)
  matrix products  35.8 us (4%)
  blocking collectives  28.9 us (3%)
  other arithmetic  18.4 us (2%)
  between operations  13.5 us (1%)
    all_gather x1, waiting for transfers between devices, per_device(): lax.all_gather(w_in, 'seq', axis=1, tiled=True)  838 us
    all_gather x1, waiting for transfers between devices, per_device(): features = lax.all_gather(inputs, 'ch', axis=1, tiled=True)  38.1 us
    all_gather x2, blocking collectives, carried_in(): gathered = jax.tree.map(lambda a: lax.all_gather(a, axis), part)  28.9 us
    dot_general x1, matrix products, per_device(): jnp.einsum('td,kdc->ktc', features, lax.all_gather(w_in, 'seq', axis=1, t...  21.8 us
  transfers between devices with their start and end apart: 3, of which 2 were waited for; matrix products, arithmetic and copies ran while one was open for 0% of the time, Pallas kernels for 0%

commit v1 on v0

--- a/solution.py
+++ b/solution.py
@@ -29,17 +29,26 @@
     return (earlier[0] * later[0], earlier[1] * later[0] + later[1])
 
 
+def project(inputs, w_in):
+    tok_rows = inputs.shape[0]
+    n_seq = lax.axis_size("seq")
+    n_ch = lax.axis_size("ch")
+    features = lax.all_gather(inputs, "ch", axis=1, tiled=True)
+    piece = features.shape[1] // (n_seq * n_ch)
+    features = features.reshape(tok_rows, n_seq, n_ch, piece)
+    mine = lax.dynamic_index_in_dim(features, lax.axis_index("ch"), 2, False)
+    rows = lax.all_to_all(mine, "seq", 1, 0, tiled=True)
+    rows = rows.reshape(n_seq * tok_rows, piece)
+    block = lax.all_gather(rows, "ch", axis=1, tiled=True)
+    partial = jnp.einsum("td,kdc->ktc", block, w_in, preferred_element_type=jnp.float32)
+    return lax.psum_scatter(partial, "seq", scatter_dimension=1, tiled=True)
+
+
 def per_device(inputs, w_in, short_filter, rates, residues, skip):
     tok_rows = inputs.shape[0]
     width = w_in.shape[2]
     modes = rates.shape[0]
-    features = lax.all_gather(inputs, "ch", axis=1, tiled=True)
-    proj = jnp.einsum(
-        "td,kdc->ktc",
-        features,
-        lax.all_gather(w_in, "seq", axis=1, tiled=True),
-        preferred_element_type=jnp.float32,
-    ).astype(jnp.bfloat16)
+    proj = project(inputs, w_in).astype(jnp.bfloat16)
     prior = passed_along(proj[:, tok_rows - (TAPS - 1) :, :], "seq", 1)
     padded = jnp.concatenate([prior, proj], axis=1).astype(jnp.float32)
     mixed = jnp.zeros((3, tok_rows, width), jnp.float32)

time: 980 us -> 416 us (0.42)
  waiting for transfers between devices: 877 us -> 288 us
  blocking collectives: 28.9 us -> 48.1 us
    all_gather x2, waiting for transfers between devices: 876 us -> 76.8 us  [the longest x1 41.3 us: project(): features = lax.all_gather(inputs, 'ch', axis=1, tiled=True)]
    reduce_scatter x0 -> x1, waiting for transfers between devices: none -> 211 us  [project(): return lax.psum_scatter(partial, 'seq', scatter_dimension=1, tiled=True)]
    all_to_all x0 -> x1, blocking collectives: none -> 19.4 us  [project(): rows = lax.all_to_all(mine, 'seq', 1, 0, tiled=True)]
  transfers between devices with their start and end apart: 3 -> 4, of which waited for: 2 -> 3; matrix products, arithmetic and copies ran while one was open for 0% -> 0% of each run, Pallas kernels for 0% -> 0%
where the time goes in v1:
time: 416 us; the launch traced here: 415 us
  waiting for transfers between devices  288 us (69%)
  blocking collectives  48.1 us (12%)
  matrix products  32.8 us (8%)
  other arithmetic  19.6 us (5%)
  between operations  13.3 us (3%)
  local copies, waits for them, and re-layouts  8.82 us (2%)
    reduce_scatter x1, waiting for transfers between devices, project(): return lax.psum_scatter(partial, 'seq', scatter_dimension=1, tiled=True)  211 us
    all_gather x1, waiting for transfers between devices, project(): features = lax.all_gather(inputs, 'ch', axis=1, tiled=True)  41.3 us
    all_gather x1, waiting for transfers between devices, project(): block = lax.all_gather(rows, 'ch', axis=1, tiled=True)  35.6 us
    all_gather x2, blocking collectives, carried_in(): gathered = jax.tree.map(lambda a: lax.all_gather(a, axis), part)  28.7 us
    all_to_all x1, blocking collectives, project(): rows = lax.all_to_all(mine, 'seq', 1, 0, tiled=True)  19.4 us
    dot_general x1, matrix products, project(): jnp.einsum('td,kdc->ktc', block, w_in, preferred_element_type=jnp.float32)  18.9 us
    dot_general x1, matrix products, per_device(): jnp.dot(lower, rising.reshape(tok_rows, modes * width), precision=lax.Pre...  13.9 us
  transfers between devices with their start and end apart: 4, of which 3 were waited for; matrix products, arithmetic and copies ran while one was open for 0% of the time, Pallas kernels for 0%

profile of v1, /device:TPU:0, one launch (start us, length us, event | category | flops | bytes accessed | tf_op | source)
XLA Modules:
  0.0 414.5 jit_solution(5616361309072354084)
XLA Ops:
  6.5 0.7 all-gather.5.cloned.1.call-update
  7.3 0.0 all-gather.7.cloned.1.call-start
  7.3 41.3 %all-gather.5.cloned.1.call-done = bf16[256,8192]{1,0:T(8,128)(2,1)} async-done(((bf16[256,1024]{1,0:T(8,128)(2,1)}), bf16[256,8192]{1,0:T(8,128)(2,1)}) %all-gather.5.cloned.1.call-update) | async-done | bytes 4194320 | tf_op jit(solution)/shard_map/all_gather | solution.py:36
  48.6 3.6 copy.15
  52.1 1.1 constant_dynamic-slice_fusion
  53.3 0.2 copy.21
  53.4 19.4 %all_to_all.15 = bf16[256,4,256]{2,0,1:T(8,128)(2,1)} all-to-all(bf16[256,4,256]{2,0,1:T(8,128)(2,1)S(1)} %bitcast.60), channel_id=1, replica_groups=mesh['seq'=4,'ch'=8] {'seq'}, dimensions={1} | all-to-all | bytes 1048576 | tf_op jit(solution)/shard_map/all_to_all | solution.py:40
  72.8 0.0 all-gather.7.cloned.1.call-update
  72.9 0.0 reduce-scatter.2.cloned.1.call-start
  72.9 35.6 %all-gather.7.cloned.1.call-done = bf16[1024,2048]{1,0:T(8,128)(2,1)} async-done(((bf16[1024,256]{1,0:T(8,128)(2,1)}), bf16[1024,2048]{1,0:T(8,128)(2,1)}) %all-gather.7.cloned.1.call-update) | async-done | bytes 4194320 | tf_op jit(solution)/shard_map/all_gather | solution.py:42
  108.5 18.9 %convolution_bitcast_fusion = f32[3,1024,1024]{2,1,0:T(8,128)} fusion(bf16[3,2048,1024]{2,1,0:T(8,128)(2,1)} %param.9, bf16[1024,2048]{1,0:T(8,128)(2,1)} %all-gather.7.cloned.1.call-done), kind=kOutput, calls=%fused_computation.6 | convolution fusion | flops 12884901888 | bytes 29360128 | tf_op jit(solution)/shard_map/td,kdc->ktc/dot_general | solution.py:43
  127.4 0.0 reduce-scatter.2.cloned.1.call-update
  127.5 0.7 copy-done.2
  128.3 0.0 copy-done
  128.3 0.6 fusion.9
  128.9 210.6 %reduce-scatter.2.cloned.1.call-done = f32[3,256,1024]{2,1,0:T(8,128)} async-done(((f32[3,1024,1024]{2,1,0:T(8,128)}), f32[3,256,1024]{2,1,0:T(8,128)}) %reduce-scatter.2.cloned.1.call-update) | async-done | bytes 3145744 | tf_op jit(solution)/shard_map/reduce_scatter | solution.py:44
  339.5 2.1 convert_element_type.10
  341.6 3.4 collective-permute-start
  345.0 13.9 %all-gather = f32[64,1024]{1,0:T(8,128)S(1)} all-gather(f32[16,1024]{1,0:T(8,128)S(1)} %get-tuple-element.63), channel_id=2, replica_groups=mesh['seq'=4,'ch'=8] {'seq'}, dimensions={0}, use_global_device_ids=true | all-gather | bytes 327680 | tf_op jit(solution)/shard_map/all_gather | solution.py:17
  358.9 0.6 copy.16
  359.6 0.5 maximum_convert_fusion
  360.1 0.9 fusion.1
  361.0 1.2 fusion.3
  362.2 2.5 copy.14
  364.7 4.1 multiply_reduce_fusion.1
  368.8 14.8 %all-gather.1 = f32[64,1024]{1,0:T(8,128)} all-gather(f32[16,1024]{1,0:T(8,128)S(1)} %multiply_reduce_fusion.1), channel_id=3, replica_groups=mesh['seq'=4,'ch'=8] {'seq'}, dimensions={0}, use_global_device_ids=true | all-gather | bytes 327680 | tf_op jit(solution)/shard_map/all_gather | solution.py:17
  383.6 0.2 while.12
  383.8 0.9 fusion.8
  384.7 3.9 bitcast_multiply_fusion.1
  388.7 13.9 %multiply_reduce_fusion.2 = f32[256,1024]{1,0:T(8,128)} fusion(f32[16,1024,256]{2,1,0:T(8,128)S(1)} %bitcast.57, f32[16,1024]{1,0:T(8,128)S(1)} %get-tuple-element.61, f32[256]{0:T(256)S(1)} %iota_add_fusion.1, f32[16,1024]{1,0:T(8,128)S(1)} %copy-done.1), kind=kOutput, calls=%fused_computation.5 | convolution fusion | flops 12901482496 | bytes 17957888 | tf_op jit(solution)/shard_map/dot_general | solution.py:76
  402.6 2.8 multiply_reduce_fusion
  405.4 2.6 fusion.5
  (16 shorter events, 0.1 us)
Async XLA Ops:
  6.5 42.0 %all-gather.5.cloned.1.call-start = ((), (), s32[]{:S(2)}) async-start(), calls=%async_computation.2 | async-start | bytes 4718592 | tf_op jit(solution)/shard_map/all_gather | solution.py:36
  7.3 101.2 %all-gather.7.cloned.1.call-start = ((), (), s32[]{:S(2)}) async-start(), calls=%async_computation.3 | async-start | bytes 4718592 | tf_op jit(solution)/shard_map/all_gather | solution.py:42
  72.9 266.6 %reduce-scatter.2.cloned.1.call-start = ((), (), s32[]{:S(2)}) async-start(), calls=%async_computation.4 | async-start | bytes 15728640 | tf_op jit(solution)/shard_map/reduce_scatter | solution.py:44
  127.4 0.8 copy-start.2
  127.4 0.9 copy-start
  341.6 18.0 %collective-permute-start = (bf16[3,2,1024]{2,1,0:T(2,128)(2,1)S(1)}, bf16[3,2,1024]{2,1,0:T(2,128)(2,1)S(1)}, u32[]{:S(2)}, u32[]{:S(2)}) collective-permute-start(bf16[3,2,1024]{2,1,0:T(2,128)(2,1)S(1)} %slice.40), channel_id=1, source_target_pairs={{0,8},{8,16},{16,24},{1,9},{9,17},{17,25},{2,10},{10,18},{18,26},{... | collective-permute-start | bytes 36872 | tf_op jit(solution)/shard_map/ppermute | solution.py:12
  383.8 4.8 %copy-start.1 = (f32[16,1024]{1,0:T(8,128)S(1)}, f32[16,1024]{1,0:T(8,128)}, u32[]{:S(2)}) copy-start(f32[16,1024]{1,0:T(8,128)} %get-tuple-element.62) | copy-start | bytes 196612
  388.7 16.7 %copy-start.3 = (f32[1024]{0:T(1024)S(1)}, f32[1024]{0:T(1024)}, u32[]{:S(2)}) copy-start(f32[1024]{0:T(1024)} %param.13) | copy-start | bytes 12292
Sparse Core Ops, SparseCore 0:
  9.2 39.2 all-gather.4
  73.0 35.4 all-gather.6
  127.6 211.8 reduce-scatter.1

commit v2 on v1

--- a/solution.py
+++ b/solution.py
@@ -12,34 +12,25 @@
     return lax.ppermute(block, axis, route)
 
 
-def carried_in(part, axis, combine, identity):
-    place = lax.axis_index(axis)
-    gathered = jax.tree.map(lambda a: lax.all_gather(a, axis), part)
-    state = jax.tree.map(lambda a, e: jnp.zeros_like(a) + jnp.asarray(e, a.dtype), part, identity)
-
-    def one(hop, state):
-        return combine(
-            state, jax.tree.map(lambda a: lax.dynamic_index_in_dim(a, hop, 0, False), gathered)
-        )
-
-    return lax.fori_loop(0, place, one, state)
-
-
-def combine(earlier, later):
-    return (earlier[0] * later[0], earlier[1] * later[0] + later[1])
+def carried_in(end_state, decay, axis):
+    total = lax.axis_size(axis)
+    state = jnp.zeros_like(end_state)
+    for distance in range(total - 1, 0, -1):
+        state = state * decay + passed_along(end_state, axis, distance)
+    return state
 
 
 def project(inputs, w_in):
-    tok_rows = inputs.shape[0]
+    tok_rows, local = inputs.shape
     n_seq = lax.axis_size("seq")
     n_ch = lax.axis_size("ch")
-    features = lax.all_gather(inputs, "ch", axis=1, tiled=True)
-    piece = features.shape[1] // (n_seq * n_ch)
-    features = features.reshape(tok_rows, n_seq, n_ch, piece)
-    mine = lax.dynamic_index_in_dim(features, lax.axis_index("ch"), 2, False)
-    rows = lax.all_to_all(mine, "seq", 1, 0, tiled=True)
-    rows = rows.reshape(n_seq * tok_rows, piece)
+    share = tok_rows // n_ch
+    pieces = lax.all_to_all(inputs.reshape(n_ch, share, local), "ch", 0, 0, tiled=True)
+    pieces = pieces.transpose(1, 0, 2).reshape(share, n_seq, (n_ch * local) // n_seq)
+    rows = lax.all_to_all(pieces, "seq", 1, 0, tiled=True)
+    rows = rows.reshape(n_seq, share, rows.shape[-1])
     block = lax.all_gather(rows, "ch", axis=1, tiled=True)
+    block = block.reshape(n_seq * tok_rows, block.shape[-1])
     partial = jnp.einsum("td,kdc->ktc", block, w_in, preferred_element_type=jnp.float32)
     return lax.psum_scatter(partial, "seq", scatter_dimension=1, tiled=True)
 
@@ -64,8 +55,7 @@
     end_powers = jnp.exp(-rates[None, :, :] * (tok_rows - 1.0 - position)[:, None, None])
     end_state = jnp.sum(end_powers * drive[:, None, :], axis=0)
     block_decay = jnp.exp(-rates * tok_rows)
-    identity = (jnp.ones_like(block_decay), jnp.zeros_like(end_state))
-    entering = carried_in((block_decay, end_state), "seq", combine, identity)[1]
+    entering = carried_in(end_state, block_decay, "seq")
     start_powers = jnp.exp(-rates[None, :, :] * (position + 1.0)[:, None, None])
     cross = jnp.sum(start_powers * (scaled * entering)[None, :, :], axis=1)
     center = (tok_rows - 1.0) / 2.0

time: 416 us -> 380 us (0.913)
  waiting for transfers between devices: 288 us -> 247 us
  blocking collectives: 48.1 us -> 33.5 us
  starting transfers between devices: 3.48 us -> 13.2 us
  local copies, waits for them, and re-layouts: 8.82 us -> 18.2 us
    all_gather x1 -> x0, waiting for transfers between devices: 41.3 us -> none  [project(): features = lax.all_gather(inputs, 'ch', axis=1, tiled=True)]
    all_gather x2 -> x0, blocking collectives: 28.7 us -> none  [carried_in(): gathered = jax.tree.map(lambda a: lax.all_gather(a, axis), part)]
    all_to_all x1 -> x2, blocking collectives: 19.4 us -> 33.5 us  [the longest x1 18.6 us: project(): rows = lax.all_to_all(pieces, 'seq', 1, 0, tiled=True)]
    ppermute x1 -> x4, starting transfers between devices: 3.39 us -> 13.2 us  [passed_along(): return lax.ppermute(block, axis, route)]
    unnamed x13 -> x11, local copies, waits for them, and re-layouts: 7.51 us -> 0.8 us
    reduce_sum x0 -> x2, local copies, waits for them, and re-layouts: none -> 5.12 us  [the longest x1 2.58 us: per_device(): cross = jnp.sum(start_powers * (scaled * entering)[None, :, :], axis=1)]
    all_gather x0 -> x1, local copies, waits for them, and re-layouts: none -> 4.48 us  [project(): block = lax.all_gather(rows, 'ch', axis=1, tiled=True)]
  transfers between devices with their start and end apart: 4 -> 6, of which waited for: 3 -> 3; matrix products, arithmetic and copies ran while one was open for 0% -> 1% of each run, Pallas kernels for 0% -> 0%
where the time goes in v2:
time: 380 us; the launch traced here: 379 us
  waiting for transfers between devices  247 us (65%)
  blocking collectives  33.5 us (9%)
  matrix products  31.9 us (8%)
  other arithmetic  21.7 us (6%)
  local copies, waits for them, and re-layouts  18.2 us (5%)
  between operations  13.6 us (4%)
  starting transfers between devices  13.2 us (3%)
    reduce_scatter x1, waiting for transfers between devices, project(): return lax.psum_scatter(partial, 'seq', scatter_dimension=1, tiled=True)  211 us
    all_gather x1, waiting for transfers between devices, project(): block = lax.all_gather(rows, 'ch', axis=1, tiled=True)  34.5 us
    all_to_all x1, blocking collectives, project(): rows = lax.all_to_all(pieces, 'seq', 1, 0, tiled=True)  18.6 us
    dot_general x1, matrix products, project(): jnp.einsum('td,kdc->ktc', block, w_in, preferred_element_type=jnp.float32)  17.8 us
    all_to_all x1, blocking collectives, project(): lax.all_to_all(inputs.reshape(n_ch, share, local), 'ch', 0, 0, tiled=True)  14.9 us
    dot_general x1, matrix products, per_device(): jnp.dot(lower, rising.reshape(tok_rows, modes * width), precision=lax.Pre...  14.1 us
    ppermute x4, starting transfers between devices, passed_along(): return lax.ppermute(block, axis, route)  13.2 us
  transfers between devices with their start and end apart: 6, of which 3 were waited for; matrix products, arithmetic and copies ran while one was open for 1% of the time, Pallas kernels for 0%

profile of v2, /device:TPU:0, one launch (start us, length us, event | category | flops | bytes accessed | tf_op | source)
XLA Modules:
  0.0 379.0 jit_solution(15950338442145141932)
XLA Ops:
  6.5 14.9 %all_to_all.20 = bf16[8,32,1024]{2,1,0:T(8,128)(2,1)S(1)} all-to-all(bf16[8,32,1024]{2,1,0:T(8,128)(2,1)} %bitcast.45), channel_id=1, replica_groups=mesh['seq'=4,'ch'=8] {'ch'}, dimensions={0} | all-to-all | bytes 1048576 | tf_op jit(solution)/shard_map/all_to_all | solution.py:28
  21.4 0.3 copy.16
  21.7 0.4 reshape.48
  22.1 0.3 copy.17
  22.4 18.6 %all_to_all.21 = bf16[32,4,2048]{2,0,1:T(8,128)(2,1)S(1)} all-to-all(bf16[32,4,2048]{2,0,1:T(8,128)(2,1)S(1)} %copy.17), channel_id=1, replica_groups=mesh['seq'=4,'ch'=8] {'seq'}, dimensions={1} | all-to-all | bytes 1048576 | tf_op jit(solution)/shard_map/all_to_all | solution.py:30
  41.0 1.2 copy.18
  42.3 34.5 %all-gather.3.cloned.1.call-done = bf16[4,256,1,2048]{3,0,2,1:T(4,128)(2,1)} async-done(((bf16[4,32,1,2048]{3,0,2,1:T(4,128)(2,1)}), bf16[4,256,1,2048]{3,0,2,1:T(4,128)(2,1)}) %all-gather.3.cloned.1.call-update) | async-done | bytes 4194320 | tf_op jit(solution)/shard_map/all_gather | solution.py:32
  76.8 4.5 %copy.19 = bf16[4,256,1,2048]{3,1,0,2:T(8,128)(2,1)S(1)} copy(bf16[4,256,1,2048]{3,0,2,1:T(4,128)(2,1)} %all-gather.3.cloned.1.call-done) | data formatting | bytes 8388608 | tf_op jit(solution)/shard_map/all_gather | solution.py:32
  81.3 17.8 %convolution_bitcast_fusion = f32[3,1024,1024]{1,2,0:T(8,128)} fusion(bf16[3,2048,1024]{2,1,0:T(8,128)(2,1)} %param.7, bf16[1024,2048,1]{1,0,2:T(8,128)(2,1)S(1)} %bitcast.41), kind=kOutput, calls=%fused_computation.4 | convolution fusion | flops 12884901888 | bytes 29360128 | tf_op jit(solution)/shard_map/td,kdc->ktc/dot_general | solution.py:34
  99.2 0.8 copy-done.2
  100.0 211.2 %reduce-scatter.2.cloned.1.call-done = f32[3,256,1024]{1,2,0:T(8,128)} async-done(((f32[3,1024,1024]{1,2,0:T(8,128)}), f32[3,256,1024]{1,2,0:T(8,128)}) %reduce-scatter.2.cloned.1.call-update) | async-done | bytes 3145744 | tf_op jit(solution)/shard_map/reduce_scatter | solution.py:35
  311.2 2.0 convert_element_type.10
  313.2 0.3 slice.40
  313.5 0.3 copy.21
  313.8 3.6 collective-permute-start
  317.5 1.1 collective-permute-done
  318.6 0.4 copy.22
  319.0 1.0 maximum_convert_fusion
  320.0 3.2 fusion
  323.2 1.1 fusion.2
  324.3 2.6 copy.23
  326.9 4.2 %multiply_reduce_fusion.1 = f32[16,1024]{1,0:T(8,128)S(1)} fusion(f32[256]{0:T(256)S(1)} %iota_subtract_fusion, f32[256,1024]{1,0:T(8,128)} %copy.23, f32[16,1024]{1,0:T(8,128)S(1)} %neg.3), kind=kLoop, calls=%fused_computation.2 | loop fusion | flops 12566528 | bytes 1180672 | tf_op jit(solution)/shard_map/reduce_sum | solution.py:56
  331.0 5.8 %collective-permute-start.1 = (f32[16,1024]{1,0:T(8,128)S(1)}, f32[16,1024]{1,0:T(8,128)S(1)}, u32[]{:S(2)}, u32[]{:S(2)}) collective-permute-start(f32[16,1024]{1,0:T(8,128)S(1)} %multiply_reduce_fusion.1), channel_id=1, source_target_pairs={{0,24},{1,25},{2,26},{3,27},{4,28},{5,29},{6,30},{7,31}} | collective-permute-start | bytes 196616 | tf_op jit(solution)/shard_map/ppermute | solution.py:12
  336.9 1.3 collective-permute-start.2
  338.2 2.5 collective-permute-start.3
  340.7 3.8 bitcast_multiply_fusion
  344.6 14.1 %multiply_reduce_fusion.2 = f32[256,1024]{1,0:T(8,128)} fusion(f32[16,1024,256]{2,1,0:T(8,128)S(1)} %bitcast.40, f32[16,1024]{1,0:T(8,128)S(1)} %get-tuple-element.6, f32[256]{0:T(256)S(1)} %iota_add_fusion.1, f32[16,1024]{1,0:T(8,128)S(1)} %neg.3), kind=kOutput, calls=%fused_computation.3 | convolution fusion | flops 12901482496 | bytes 17957888 | tf_op jit(solution)/shard_map/dot_general | solution.py:66
  358.6 2.5 copy.25
  361.2 3.8 multiply_reduce_fusion
  364.9 2.6 copy.26
  367.5 2.6 fusion.4
  370.1 2.0 copy.27
  (23 shorter events, 0.3 us)
Async XLA Ops:
  6.5 70.3 %all-gather.3.cloned.1.call-start = ((), (), s32[]{:S(2)}) async-start(), calls=%async_computation.4 | async-start | bytes 4718592 | tf_op jit(solution)/shard_map/all_gather | solution.py:32
  42.3 268.9 %reduce-scatter.2.cloned.1.call-start = ((), (), s32[]{:S(2)}) async-start(), calls=%async_computation.3 | async-start | bytes 15728640 | tf_op jit(solution)/shard_map/reduce_scatter | solution.py:35
  99.1 0.8 copy-start.2
  99.1 218.3 %copy-start = (f32[16,1024]{1,0:T(8,128)S(1)}, f32[16,1024]{1,0:T(8,128)}, u32[]{:S(2)}) copy-start(f32[16,1024]{1,0:T(8,128)} %param.9) | copy-start | bytes 196612
  313.8 4.8 %collective-permute-start = (bf16[3,2,1024]{2,1,0:T(2,128)(2,1)S(1)}, bf16[3,2,1024]{2,1,0:T(2,128)(2,1)S(1)}, u32[]{:S(2)}, u32[]{:S(2)}) collective-permute-start(bf16[3,2,1024]{2,1,0:T(2,128)(2,1)S(1)} %copy.21), channel_id=1, source_target_pairs={{0,8},{8,16},{16,24},{1,9},{9,17},{17,25},{2,10},{10,18},{18,26},{... | collective-permute-start | bytes 36872 | tf_op jit(solution)/shard_map/ppermute | solution.py:12
  326.9 17.6 %copy-start.1 = (f32[16,1024]{1,0:T(8,128)S(1)}, f32[16,1024]{1,0:T(8,128)}, u32[]{:S(2)}) copy-start(f32[16,1024]{1,0:T(8,128)} %param.10) | copy-start | bytes 196612
  331.0 13.4 %collective-permute-start.1 = (f32[16,1024]{1,0:T(8,128)S(1)}, f32[16,1024]{1,0:T(8,128)S(1)}, u32[]{:S(2)}, u32[]{:S(2)}) collective-permute-start(f32[16,1024]{1,0:T(8,128)S(1)} %multiply_reduce_fusion.1), channel_id=1, source_target_pairs={{0,24},{1,25},{2,26},{3,27},{4,28},{5,29},{6,30},{7,31}} | collective-permute-start | bytes 196616 | tf_op jit(solution)/shard_map/ppermute | solution.py:12
  336.9 7.6 %collective-permute-start.2 = (f32[16,1024]{1,0:T(8,128)S(1)}, f32[16,1024]{1,0:T(8,128)S(1)}, u32[]{:S(2)}, u32[]{:S(2)}) collective-permute-start(f32[16,1024]{1,0:T(8,128)S(1)} %multiply_reduce_fusion.1), channel_id=1, source_target_pairs={{0,16},{8,24},{1,17},{9,25},{2,18},{10,26},{3,19},{11,27},{4,20},{... | collective-permute-start | bytes 196616 | tf_op jit(solution)/shard_map/ppermute | solution.py:12
  338.2 6.3 %collective-permute-start.3 = (f32[16,1024]{1,0:T(8,128)S(1)}, f32[16,1024]{1,0:T(8,128)S(1)}, u32[]{:S(2)}, u32[]{:S(2)}) collective-permute-start(f32[16,1024]{1,0:T(8,128)S(1)} %multiply_reduce_fusion.1), channel_id=1, source_target_pairs={{0,8},{8,16},{16,24},{1,9},{9,17},{17,25},{2,10},{10,18},{18,26},{... | collective-permute-start | bytes 196616 | tf_op jit(solution)/shard_map/ppermute | solution.py:12
  344.6 23.0 %copy-start.3 = (f32[1024]{0:T(1024)S(1)}, f32[1024]{0:T(1024)}, u32[]{:S(2)}) copy-start(f32[1024]{0:T(1024)} %param.11) | copy-start | bytes 12292
Sparse Core Ops, SparseCore 0:
  42.4 34.4 all-gather.2
  99.3 211.8 reduce-scatter.1
